TPU v7x, 128 devices: a whole 4x4x4 slice. The times are simulated.
128 devices in a mesh: enc: 16 (over z, y), dp: 2 (over x_hi), tensor: 4 (over x_lo, core).
Axes of the slice: x: 4 (x_hi: 2, x_lo: 2; x = x_hi * 2 + x_lo), y: 4, z: 4, core: 2. Of those that a mesh axis runs over, the one named last changes fastest.
Arguments:
- hidden_in: bfloat16 [3, 64, 4096], P(None, 'dp', 'enc')
- self_cache: bfloat16 [64, 8, 2, 2048], P(('dp', 'enc'), None, None, 'tensor'), may hold values from -6 to 6
- src_pool: bfloat16 [64, 24, 2, 2048], P(('dp', 'enc'), None, None, 'tensor'), may hold values from -6 to 6
- assign: int32 [64], replicated, may hold values from 0 to 63, as said below
- src_len: int32 [64], replicated, may hold values from 1 to 24, 768 in all
- positions: int32 [64], replicated, may hold values from 1 to 8, 256 in all
- gain_self: float32 [4096], P('enc'), may hold values from 0.1 to 1.9
- w_qkv: bfloat16 [4096, 3, 2048], P('enc', None, 'tensor'), may hold values from -0.09375 to 0.09375
- w_out_self: bfloat16 [2048, 4096], P('tensor', 'enc'), may hold values from -0.125 to 0.125
- gain_cross: float32 [4096], P('enc'), may hold values from 0.1 to 1.9
- w_q_cross: bfloat16 [4096, 2048], P('enc', 'tensor'), may hold values from -0.09375 to 0.09375
- w_out_cross: bfloat16 [2048, 4096], P('tensor', 'enc'), may hold values from -0.125 to 0.125
Outputs:
- layer_out: bfloat16 [3, 64, 4096], P(None, 'dp', 'enc')
Inputs may be any that keep to these rules, and one draw needn't show every extreme that they name: `assign`: a permutation of the 64 sources; with blocks of 2 consecutive sequences or sources numbered d * 16 + e, the 2 sequences of block d * 16 + e read exactly one source from each block d2 * 16 + e that has the same e.
All inputs are finite; a program needn't handle non-finite values.
Results may differ from a plain program's by a relative error of at most 0.008.
Values may be sent and summed in bfloat16 or wider, within the bound.
No kernel may reach another device: no remote copies, remote signals or barrier semaphores. Data moves between devices by JAX's collectives and lax.ppermute only.
A program may use at most 64 MiB of HBM per device.

v0:
```python
import math
import jax
import jax.numpy as jnp
from jax import lax
from jax.sharding import PartitionSpec as P

D = 4096
DK = 256
STEPS = 3
EPSILON = 1e-06


def row_norm(rows_in, gain_vec):
    squares = lax.psum(jnp.sum(rows_in * rows_in, axis=1), "enc")
    return (rows_in * lax.rsqrt(squares / D + EPSILON)[:, None] * gain_vec[None, :]).astype(
        jnp.bfloat16
    )


def score_weight(scores):
    return jnp.exp(scores).astype(jnp.bfloat16)


def attend(query_rows, key_rows, value_rows, usable):
    count = query_rows.shape[0]
    head_count = query_rows.shape[1] // DK
    query_heads = query_rows.reshape(count, head_count, DK)
    key_heads = key_rows.reshape(count, key_rows.shape[1], head_count, DK)
    value_heads = value_rows.reshape(count, value_rows.shape[1], head_count, DK)
    scores = jnp.einsum(
        "nhd,nlhd->nhl", query_heads, key_heads, preferred_element_type=jnp.float32
    ) * (1.0 / math.sqrt(DK))
    weights = jnp.where(usable[:, None, :], score_weight(scores), jnp.zeros((), jnp.bfloat16))
    weighted = jnp.einsum("nhl,nlhd->nhd", weights, value_heads, preferred_element_type=jnp.float32)
    return (weighted, jnp.sum(weights.astype(jnp.float32), axis=-1))


def combine_heads(context, weight_out):
    partial_out = jnp.dot(context, weight_out, preferred_element_type=jnp.float32)
    return lax.psum(partial_out, "tensor")


def on_device(
    hidden_in,
    self_cache,
    src_pool,
    assign,
    src_len,
    positions,
    gain_self,
    w_qkv,
    w_out_self,
    gain_cross,
    w_q_cross,
    w_out_cross,
):
    dp_count = lax.axis_size("dp")
    enc_count = lax.axis_size("enc")
    seq_dev = self_cache.shape[0]
    per_pair = seq_dev // dp_count
    cache_len = self_cache.shape[1]
    source_len = src_pool.shape[1]
    enc_at = lax.axis_index("enc")
    dp_at = lax.axis_index("dp")
    block_at = dp_at * enc_count + enc_at
    slot_index = jnp.arange(seq_dev, dtype=jnp.int32)
    my_slots = block_at * seq_dev + slot_index
    my_positions = jnp.take(positions, my_slots)
    my_sources = jnp.take(assign, my_slots)
    place_at = jnp.arange(cache_len, dtype=jnp.int32)
    cache_usable = place_at[None, :] < my_positions[:, None]
    token_at = jnp.arange(source_len, dtype=jnp.int32)
    assign_view = assign.reshape(dp_count, enc_count, seq_dev)
    assign_grid = jnp.take(assign_view, enc_at, axis=1)
    owners = assign_grid // (seq_dev * enc_count)
    earlier = (owners[:, None, :] == owners[:, :, None]) & (
        slot_index[None, None, :] < slot_index[None, :, None]
    )
    slot_rank = jnp.sum(earlier.astype(jnp.int32), axis=2)
    recv_rows = jnp.take(owners, dp_at, axis=0) * per_pair + jnp.take(slot_rank, dp_at, axis=0)
    picked = (owners == dp_at)[:, :, None] & (
        slot_rank[:, :, None] == jnp.arange(per_pair, dtype=jnp.int32)[None, None, :]
    )
    chosen = jnp.sum(jnp.where(picked, (assign_grid % seq_dev)[:, :, None], 0), axis=1)
    chosen_flat = chosen.reshape(-1)
    outgoing = jnp.take(src_pool, chosen_flat, axis=0)
    arrived = lax.all_to_all(outgoing, "dp", split_axis=0, concat_axis=0, tiled=True)
    cross_kv = jnp.take(arrived, recv_rows, axis=0)
    cross_usable = token_at[None, :] < jnp.take(src_len, my_sources)[:, None]
    key_list = []
    value_list = []
    results = []
    for step_at in range(STEPS):
        current = hidden_in[step_at].astype(jnp.float32)
        normed = row_norm(current, gain_self)
        projected = jnp.einsum("sd,dcw->scw", normed, w_qkv, preferred_element_type=jnp.float32)
        own_proj = lax.psum_scatter(projected, "enc", scatter_dimension=0, tiled=True).astype(
            jnp.bfloat16
        )
        query_rows = own_proj[:, 0]
        key_list.append(own_proj[:, 1])
        value_list.append(own_proj[:, 2])
        weighted, totals = attend(
            query_rows, self_cache[:, :, 0], self_cache[:, :, 1], cache_usable
        )
        head_count = weighted.shape[1]
        query_heads = query_rows.astype(jnp.float32).reshape(seq_dev, head_count, DK)
        for key_new, value_new in zip(key_list, value_list):
            scores = jnp.sum(
                query_heads * key_new.astype(jnp.float32).reshape(seq_dev, head_count, DK), axis=-1
            ) * (1.0 / math.sqrt(DK))
            weights = score_weight(scores).astype(jnp.float32)
            weighted = weighted + weights[:, :, None] * value_new.astype(jnp.float32).reshape(
                seq_dev, head_count, DK
            )
            totals = totals + weights
        context = (
            (weighted / totals[:, :, None]).reshape(seq_dev, head_count * DK).astype(jnp.bfloat16)
        )
        context_all = lax.all_gather(context, "enc", axis=0, tiled=True)
        residual = current + combine_heads(context_all, w_out_self)
        normed_cross = row_norm(residual, gain_cross)
        cross_query = jnp.dot(normed_cross, w_q_cross, preferred_element_type=jnp.float32)
        own_query = lax.psum_scatter(cross_query, "enc", scatter_dimension=0, tiled=True).astype(
            jnp.bfloat16
        )
        weighted, totals = attend(own_query, cross_kv[:, :, 0], cross_kv[:, :, 1], cross_usable)
        context = (
            (weighted / totals[:, :, None]).reshape(seq_dev, head_count * DK).astype(jnp.bfloat16)
        )
        context_all = lax.all_gather(context, "enc", axis=0, tiled=True)
        output_rows = residual + combine_heads(context_all, w_out_cross)
        results.append(output_rows.astype(jnp.bfloat16))
    return jnp.stack(results)


def solution(mesh):
    in_specs = (
        P(None, "dp", "enc"),
        P(("dp", "enc"), None, None, "tensor"),
        P(("dp", "enc"), None, None, "tensor"),
        P(),
        P(),
        P(),
        P("enc"),
        P("enc", None, "tensor"),
        P("tensor", "enc"),
        P("enc"),
        P("enc", "tensor"),
        P("tensor", "enc"),
    )
    out_specs = P(None, "dp", "enc")
    return jax.shard_map(
        on_device, mesh=mesh, in_specs=in_specs, out_specs=out_specs, check_vma=False
    )
```

profile of v0, /device:TPU:1, one launch (start us, length us, event | category | flops | bytes accessed | tf_op | source)
XLA Modules:
  0.0 470.3 jit_solution(5215867503166297110)
XLA Ops:
  6.6 0.7 copy-done.1
  7.4 0.2 fusion.80
  7.8 0.6 gather_fusion.1
  8.5 0.2 copy-done.12
  8.7 0.7 gather_fusion.3
  9.4 0.8 broadcast_select_fusion.1
  10.2 5.0 %all-to-all-start = ((bf16[2,24,2,512]{3,2,1,0:T(2,128)(2,1)}), bf16[2,24,2,512]{3,2,1,0:T(2,128)(2,1)S(1)}, u32[]{:S(2)}, u32[]{:S(2)}) async-start(bf16[2,24,2,512]{3,2,1,0:T(2,128)(2,1)} %broadcast_select_fusion.1), calls=%async_computation | async-start | bytes 196608 | tf_op jit(solution)/shard_map/all_to_all | solution.py:87
  15.3 34.7 %all-reduce.9 = (f32[32]{0:T(128)S(1)}, f32[32]{0:T(128)S(1)}, f32[32]{0:T(128)S(1)}) all-reduce(f32[32]{0:T(128)S(1)} %get-tuple-element.35, f32[32]{0:T(128)S(1)} %get-tuple-element.36, f32[32]{0:T(128)S(1)} %get-tuple-element.37), channel_id=1, replica_groups=mesh['enc'=16,'dp'=2,'tensor'=4] {'enc'}, use_global_device_ids=true, to_apply=%region_1.3 | all-reduce | flops 96 | bytes 768 | tf_op jit(solution)/shard_map/psum | solution.py:14
  50.0 0.7 copy-done.14
  50.7 0.3 fusion.34
  51.0 0.3 fusion.37
  51.3 0.3 fusion.40
  51.6 0.7 copy-done.15
  52.2 0.6 dynamic-slice.11
  53.5 62.2 %all-reduce.20 = (bf16[32,3,512]{2,0,1:T(8,128)(2,1)S(1)}, bf16[32,3,512]{2,0,1:T(8,128)(2,1)S(1)}, bf16[32,3,512]{2,0,1:T(8,128)(2,1)S(1)}) all-reduce(f32[32,3,512]{2,0,1:T(8,128)S(1)} %fusion.40, f32[32,3,512]{2,0,1:T(8,128)S(1)} %fusion.34, f32[32,3,512]{2,0,1:T(8,128)S(1)} %fusion.37), channel_id=2, replica_groups=mesh['enc'=16,'dp'=2,'tensor'=4] {'enc'}, use_global_device_ids=true, to_apply=%region_2.4.clone | all-reduce | flops 147456 | bytes 884736
  116.0 0.6 copy-done.11
  117.1 0.4 copy-done.2
  117.5 0.6 gather_fusion
  119.0 15.2 %all-gather = bf16[16,2,512]{2,1,0:T(2,128)(2,1)S(1)} all-gather(bf16[1,2,512]{2,1,0:T(2,128)(2,1)S(1)} %reshape.380), channel_id=1, replica_groups=mesh['enc'=16,'dp'=2,'tensor'=4] {'enc'}, dimensions={0}, use_global_device_ids=true | all-gather | bytes 34816 | tf_op jit(solution)/shard_map/all_gather | solution.py:120
  134.2 18.0 %all-gather.2 = bf16[16,2,512]{2,1,0:T(2,128)(2,1)S(1)} all-gather(bf16[1,2,512]{2,1,0:T(2,128)(2,1)S(1)} %reshape.384), channel_id=1, replica_groups=mesh['enc'=16,'dp'=2,'tensor'=4] {'enc'}, dimensions={0}, use_global_device_ids=true | all-gather | bytes 34816 | tf_op jit(solution)/shard_map/all_gather | solution.py:120
  152.3 0.8 fusion.102
  153.1 0.8 fusion.105
  153.8 15.4 %all-gather.4 = bf16[16,2,512]{2,1,0:T(2,128)(2,1)S(1)} all-gather(bf16[1,2,512]{2,1,0:T(2,128)(2,1)S(1)} %reshape.388), channel_id=1, replica_groups=mesh['enc'=16,'dp'=2,'tensor'=4] {'enc'}, dimensions={0}, use_global_device_ids=true | all-gather | bytes 34816 | tf_op jit(solution)/shard_map/all_gather | solution.py:120
  169.3 0.8 fusion.108
  170.1 0.5 copy-done.3
  170.7 0.6 gather_fusion.2
  171.4 0.7 gather_fusion.4
  172.2 0.2 broadcast_select_fusion
  172.3 0.4 slice_reduce_fusion.1
  172.8 70.9 %all-reduce.19.cloned.1.call-done = (f32[32,256]{1,0:T(8,128)}, f32[32,256]{1,0:T(8,128)}, f32[32,256]{1,0:T(8,128)}) async-done(((f32[32,256]{1,0:T(8,128)}, f32[32,256]{1,0:T(8,128)}, f32[32,256]{1,0:T(8,128)}), (f32[32,256]{1,0:T(8,128)}, f32[32,256]{1,0:T(8,128)}, f32[32,256]{1,0:T(8,128)})) %all-reduce.19.cloned.1.call-update) | async-done | bytes 98320 | tf_op jit(solution)/shard_map/psum | solution.py:40
  243.7 1.0 multiply_reduce_fusion.2
  244.6 33.3 %all-reduce.7 = (f32[32]{0:T(128)S(1)}, f32[32]{0:T(128)S(1)}, f32[32]{0:T(128)S(1)}) all-reduce(f32[32]{0:T(128)S(1)} %get-tuple-element.34, f32[32]{0:T(128)S(1)} %get-tuple-element.33, f32[32]{0:T(128)S(1)} %get-tuple-element.32), channel_id=1, replica_groups=mesh['enc'=16,'dp'=2,'tensor'=4] {'enc'}, use_global_device_ids=true, to_apply=%region_34.38 | all-reduce | flops 96 | bytes 768 | tf_op jit(solution)/shard_map/psum | solution.py:14
  278.0 0.7 copy-done.13
  278.7 0.2 fusion.27
  278.9 0.6 copy-done.9
  279.4 0.2 fusion.29
  279.6 0.6 copy-done.10
  280.2 0.2 fusion.31
  280.4 57.3 %all-reduce.21 = (bf16[32,512]{1,0:T(8,128)(2,1)S(1)}, bf16[32,512]{1,0:T(8,128)(2,1)S(1)}, bf16[32,512]{1,0:T(8,128)(2,1)S(1)}) all-reduce(f32[32,512]{1,0:T(8,128)S(1)} %fusion.31, f32[32,512]{1,0:T(8,128)S(1)} %fusion.29, f32[32,512]{1,0:T(8,128)S(1)} %fusion.27), channel_id=7, replica_groups=mesh['enc'=16,'dp'=2,'tensor'=4] {'enc'}, use_global_device_ids=true, to_apply=%region_35.39.clone | all-reduce | flops 49152 | bytes 294912
  338.5 16.3 %all-gather.1 = bf16[16,2,512]{2,1,0:T(2,128)(2,1)S(1)} all-gather(bf16[1,2,512]{2,1,0:T(2,128)(2,1)S(1)} %reshape.382), channel_id=1, replica_groups=mesh['enc'=16,'dp'=2,'tensor'=4] {'enc'}, dimensions={0}, use_global_device_ids=true | all-gather | bytes 34816 | tf_op jit(solution)/shard_map/all_gather | solution.py:131
  355.0 17.4 %all-gather.3 = bf16[16,2,512]{2,1,0:T(2,128)(2,1)S(1)} all-gather(bf16[1,2,512]{2,1,0:T(2,128)(2,1)S(1)} %reshape.386), channel_id=1, replica_groups=mesh['enc'=16,'dp'=2,'tensor'=4] {'enc'}, dimensions={0}, use_global_device_ids=true | all-gather | bytes 34816 | tf_op jit(solution)/shard_map/all_gather | solution.py:131
  372.5 0.8 fusion.103
  373.2 0.8 fusion.106
  374.2 15.7 %all-gather.5 = bf16[16,2,512]{2,1,0:T(2,128)(2,1)S(1)} all-gather(bf16[1,2,512]{2,1,0:T(2,128)(2,1)S(1)} %reshape.390), channel_id=1, replica_groups=mesh['enc'=16,'dp'=2,'tensor'=4] {'enc'}, dimensions={0}, use_global_device_ids=true | all-gather | bytes 34816 | tf_op jit(solution)/shard_map/all_gather | solution.py:131
  389.9 0.8 fusion.109
  390.7 71.3 %all-reduce.17.cloned.1.call-done = (f32[32,256]{1,0:T(8,128)}, f32[32,256]{1,0:T(8,128)}, f32[32,256]{1,0:T(8,128)}) async-done(((f32[32,256]{1,0:T(8,128)}, f32[32,256]{1,0:T(8,128)}, f32[32,256]{1,0:T(8,128)}), (f32[32,256]{1,0:T(8,128)}, f32[32,256]{1,0:T(8,128)}, f32[32,256]{1,0:T(8,128)})) %all-reduce.17.cloned.1.call-update) | async-done | bytes 98320 | tf_op jit(solution)/shard_map/psum | solution.py:40
  462.1 0.8 fusion.28
  462.9 0.6 pad_maximum_fusion
  (109 shorter events, 3.5 us)
Async XLA Ops:
  6.5 43.5 %copy-start = (bf16[256,3,512]{2,0,1:T(8,128)(2,1)S(1)}, bf16[256,3,512]{2,0,1:T(8,128)(2,1)}, u32[]{:S(2)}) copy-start(bf16[256,3,512]{2,0,1:T(8,128)(2,1)} %param.25) | copy-start | bytes 2359300
  6.6 0.7 copy-start.1
  7.8 0.9 copy-start.12
  10.2 5.0 %copy-start.7 = (bf16[3,32,256]{2,1,0:T(8,128)(2,1)S(1)}, bf16[3,32,256]{2,1,0:T(8,128)(2,1)}, u32[]{:S(2)}) copy-start(bf16[3,32,256]{2,1,0:T(8,128)(2,1)} %param.18) | copy-start | bytes 147460
  10.2 161.2 %all-to-all-start = ((bf16[2,24,2,512]{3,2,1,0:T(2,128)(2,1)}), bf16[2,24,2,512]{3,2,1,0:T(2,128)(2,1)S(1)}, u32[]{:S(2)}, u32[]{:S(2)}) async-start(bf16[2,24,2,512]{3,2,1,0:T(2,128)(2,1)} %broadcast_select_fusion.1), calls=%async_computation | async-start | bytes 196608 | tf_op jit(solution)/shard_map/all_to_all | solution.py:87
  15.2 228.5 %all-reduce.19.cloned.1.call-start = ((), (), s32[]{:S(2)}) async-start(), calls=%async_computation.2 | async-start | bytes 196608 | tf_op jit(solution)/shard_map/psum | solution.py:40
  50.0 0.7 copy-start.14
  51.6 0.7 copy-start.15
  115.8 0.8 copy-start.11
  116.9 0.7 copy-start.2
  118.2 34.1 %copy-start.4 = (bf16[512,256]{1,0:T(8,128)(2,1)S(1)}, bf16[512,256]{1,0:T(8,128)(2,1)}, u32[]{:S(2)}) copy-start(bf16[512,256]{1,0:T(8,128)(2,1)} %param.26) | copy-start | bytes 786436
  170.0 0.7 copy-start.3
  170.0 292.0 %all-reduce.17.cloned.1.call-start = ((), (), s32[]{:S(2)}) async-start(), calls=%async_computation.1 | async-start | bytes 196608 | tf_op jit(solution)/shard_map/psum | solution.py:40
  172.3 105.7 %copy-start.6 = (bf16[256,512]{1,0:T(8,128)(2,1)S(1)}, bf16[256,512]{1,0:T(8,128)(2,1)}, u32[]{:S(2)}) copy-start(bf16[256,512]{1,0:T(8,128)(2,1)} %param.28) | copy-start | bytes 786436
  243.7 34.4 %copy-start.8 = (f32[32,256]{1,0:T(8,128)S(1)}, f32[32,256]{1,0:T(8,128)}, u32[]{:S(2)}) copy-start(f32[32,256]{1,0:T(8,128)} %get-tuple-element.64) | copy-start | bytes 98308
  278.0 0.7 copy-start.13
  278.7 0.8 copy-start.9
  279.4 0.8 copy-start.10
  337.9 34.6 %copy-start.5 = (bf16[512,256]{1,0:T(8,128)(2,1)S(1)}, bf16[512,256]{1,0:T(8,128)(2,1)}, u32[]{:S(2)}) copy-start(bf16[512,256]{1,0:T(8,128)(2,1)} %param.29) | copy-start | bytes 786436
Sparse Core Ops, SparseCore 0:
  170.2 73.4 all-reduce.18
  390.8 71.1 all-reduce.16
where the time goes:
time: 471 us; the launch traced here: 470 us
  blocking collectives  286 us (61%)
  waiting for transfers between devices  142 us (30%)
  between operations  14.4 us (3%)
  local copies, waits for them, and re-layouts  10.8 us (2%)
  matrix products  7.41 us (2%)
  starting transfers between devices  5 us (1%)
  other arithmetic  4.79 us (1%)
    psum x2, waiting for transfers between devices, combine_heads(): return lax.psum(partial_out, 'tensor')  142 us
    unnamed x2, blocking collectives  120 us
    all_gather x6, blocking collectives, on_device(): context_all = lax.all_gather(context, 'enc', axis=0, tiled=True)  98 us
    psum x2, blocking collectives, row_norm(): squares = lax.psum(jnp.sum(rows_in * rows_in, axis=1), 'enc')  68.1 us
  transfers between devices with their start and end apart: 3, of which 2 were waited for; matrix products, arithmetic and copies ran while one was open for 2% of the time, Pallas kernels for 0%

commit v1 on v0

--- a/solution.py
+++ b/solution.py
@@ -37,7 +37,7 @@
 
 def combine_heads(context, weight_out):
     partial_out = jnp.dot(context, weight_out, preferred_element_type=jnp.float32)
-    return lax.psum(partial_out, "tensor")
+    return jnp.sum(lax.all_gather(partial_out, "tensor"), axis=0)
 
 
 def on_device(

time: 471 us -> 519 us (1.10)
  blocking collectives: 286 us -> 496 us
  waiting for transfers between devices: 142 us -> 0.01 us
  between operations: 14.4 us -> 1.12 us
    psum x2 -> x0, waiting for transfers between devices: 142 us -> none  [combine_heads(): return lax.psum(partial_out, 'tensor')]
    all_gather x0 -> x6, blocking collectives: none -> 127 us  [combine_heads(): return jnp.sum(lax.all_gather(partial_out, 'tensor'), axis=0)]
    unnamed x2 -> x3, blocking collectives: 120 us -> 174 us
    psum x2 -> x3, blocking collectives: 68.1 us -> 96.8 us  [row_norm(): squares = lax.psum(jnp.sum(rows_in * rows_in, axis=1), 'enc')]
  transfers between devices with their start and end apart: 3 -> 1, of which waited for: 2 -> 0; matrix products, arithmetic and copies ran while one was open for 2% -> 1% of each run, Pallas kernels for 0% -> 0%
where the time goes in v1:
time: 519 us; the launch traced here: 518 us
  blocking collectives  496 us (96%)
  local copies, waits for them, and re-layouts  8.66 us (2%)
    unnamed x3, blocking collectives  174 us
    all_gather x6, blocking collectives, combine_heads(): return jnp.sum(lax.all_gather(partial_out, 'tensor'), axis=0)  127 us
    all_gather x6, blocking collectives, on_device(): context_all = lax.all_gather(context, 'enc', axis=0, tiled=True)  97.5 us
    psum x3, blocking collectives, row_norm(): squares = lax.psum(jnp.sum(rows_in * rows_in, axis=1), 'enc')  96.8 us
  transfers between devices with their start and end apart: 1, of which 0 were waited for; matrix products, arithmetic and copies ran while one was open for 1% of the time, Pallas kernels for 0%

profile of v1, /device:TPU:1, one launch (start us, length us, event | category | flops | bytes accessed | tf_op | source)
XLA Modules:
  0.0 517.9 jit_solution(17448926129918049210)
XLA Ops:
  0.1 0.7 copy-done.1
  0.9 0.2 fusion.89
  1.3 0.6 gather_fusion.1
  1.9 0.2 copy-done.9
  2.2 0.7 gather_fusion.3
  2.9 0.8 broadcast_select_fusion.1
  3.7 5.0 all-to-all-start
  8.8 34.7 %psum.42 = f32[32]{0:T(128)S(1)} all-reduce(f32[32]{0:T(128)S(1)} %fusion.27), channel_id=1, replica_groups=mesh['enc'=16,'dp'=2,'tensor'=4] {'enc'}, use_global_device_ids=true, to_apply=%region_1.3 | all-reduce | flops 32 | bytes 256 | tf_op jit(solution)/shard_map/psum | solution.py:14
  43.5 0.7 copy-done.11
  44.1 0.3 fusion.52
  44.4 57.1 %all-reduce.13 = bf16[32,3,512]{2,0,1:T(8,128)(2,1)S(1)} all-reduce(f32[32,3,512]{2,0,1:T(8,128)S(1)} %fusion.52), channel_id=8, replica_groups=mesh['enc'=16,'dp'=2,'tensor'=4] {'enc'}, use_global_device_ids=true, to_apply=%region_2.4.clone | all-reduce | flops 49152 | bytes 294912
  101.6 0.6 copy-done.12
  102.2 0.6 dynamic-slice.11
  103.5 0.6 copy-done.2
  104.1 0.6 gather_fusion
  105.6 15.4 %all-gather.6 = bf16[16,2,512]{2,1,0:T(2,128)(2,1)S(1)} all-gather(bf16[1,2,512]{2,1,0:T(2,128)(2,1)S(1)} %reshape.392), channel_id=1, replica_groups=mesh['enc'=16,'dp'=2,'tensor'=4] {'enc'}, dimensions={0}, use_global_device_ids=true | all-gather | bytes 34816 | tf_op jit(solution)/shard_map/all_gather | solution.py:120
  121.0 0.1 fusion.112
  121.2 32.3 %all-gather = f32[128,256]{1,0:T(8,128)S(1)} all-gather(f32[32,256]{1,0:T(8,128)S(1)} %fusion.112), channel_id=2, replica_groups=mesh['enc'=16,'dp'=2,'tensor'=4] {'tensor'}, dimensions={0}, use_global_device_ids=true | all-gather | bytes 163840 | tf_op jit(solution)/shard_map/all_gather | solution.py:40
  153.5 0.2 multiply_reduce_fusion.2
  153.6 31.0 %all-reduce.9 = (f32[32]{0:T(128)S(1)}, f32[32]{0:T(128)S(1)}) all-reduce(f32[32]{0:T(128)S(1)} %get-tuple-element.34, f32[32]{0:T(128)S(1)} %get-tuple-element.33), channel_id=1, replica_groups=mesh['enc'=16,'dp'=2,'tensor'=4] {'enc'}, use_global_device_ids=true, to_apply=%region_26.30 | all-reduce | flops 64 | bytes 512 | tf_op jit(solution)/shard_map/psum | solution.py:14
  184.7 0.3 fusion.46
  185.0 0.3 fusion.49
  185.2 59.8 %all-reduce.14 = (bf16[32,3,512]{2,0,1:T(8,128)(2,1)S(1)}, bf16[32,3,512]{2,0,1:T(8,128)(2,1)S(1)}) all-reduce(f32[32,3,512]{2,0,1:T(8,128)S(1)} %fusion.46, f32[32,3,512]{2,0,1:T(8,128)S(1)} %fusion.49), channel_id=12, replica_groups=mesh['enc'=16,'dp'=2,'tensor'=4] {'enc'}, use_global_device_ids=true, to_apply=%region_27.31.clone | all-reduce | flops 98304 | bytes 589824
  246.0 15.7 %all-gather.8 = bf16[16,2,512]{2,1,0:T(2,128)(2,1)S(1)} all-gather(bf16[1,2,512]{2,1,0:T(2,128)(2,1)S(1)} %reshape.396), channel_id=1, replica_groups=mesh['enc'=16,'dp'=2,'tensor'=4] {'enc'}, dimensions={0}, use_global_device_ids=true | all-gather | bytes 34816 | tf_op jit(solution)/shard_map/all_gather | solution.py:120
  261.8 0.1 fusion.115
  262.0 30.7 %all-gather.2 = f32[128,256]{1,0:T(8,128)S(1)} all-gather(f32[32,256]{1,0:T(8,128)S(1)} %fusion.115), channel_id=4, replica_groups=mesh['enc'=16,'dp'=2,'tensor'=4] {'tensor'}, dimensions={0}, use_global_device_ids=true | all-gather | bytes 163840 | tf_op jit(solution)/shard_map/all_gather | solution.py:40
  292.7 18.0 %all-gather.10 = bf16[16,2,512]{2,1,0:T(2,128)(2,1)S(1)} all-gather(bf16[1,2,512]{2,1,0:T(2,128)(2,1)S(1)} %reshape.400), channel_id=1, replica_groups=mesh['enc'=16,'dp'=2,'tensor'=4] {'enc'}, dimensions={0}, use_global_device_ids=true | all-gather | bytes 34816 | tf_op jit(solution)/shard_map/all_gather | solution.py:120
  310.7 0.1 fusion.118
  310.9 11.0 %all-gather.4 = f32[128,256]{1,0:T(8,128)S(1)} all-gather(f32[32,256]{1,0:T(8,128)S(1)} %fusion.118), channel_id=6, replica_groups=mesh['enc'=16,'dp'=2,'tensor'=4] {'tensor'}, dimensions={0}, use_global_device_ids=true | all-gather | bytes 163840 | tf_op jit(solution)/shard_map/all_gather | solution.py:40
  322.1 31.0 %all-reduce.7 = (f32[32]{0:T(128)S(1)}, f32[32]{0:T(128)S(1)}, f32[32]{0:T(128)S(1)}) all-reduce(f32[32]{0:T(128)S(1)} %get-tuple-element.36, f32[32]{0:T(128)S(1)} %get-tuple-element.35, f32[32]{0:T(128)S(1)} %get-tuple-element.32), channel_id=1, replica_groups=mesh['enc'=16,'dp'=2,'tensor'=4] {'enc'}, use_global_device_ids=true, to_apply=%region_34.38 | all-reduce | flops 96 | bytes 768 | tf_op jit(solution)/shard_map/psum | solution.py:14
  353.1 0.7 copy-done.10
  353.8 0.2 fusion.42
  354.0 0.2 fusion.43
  354.2 0.2 fusion.44
  354.4 57.4 %all-reduce.15 = (bf16[32,512]{1,0:T(8,128)(2,1)S(1)}, bf16[32,512]{1,0:T(8,128)(2,1)S(1)}, bf16[32,512]{1,0:T(8,128)(2,1)S(1)}) all-reduce(f32[32,512]{1,0:T(8,128)S(1)} %fusion.44, f32[32,512]{1,0:T(8,128)S(1)} %fusion.43, f32[32,512]{1,0:T(8,128)S(1)} %fusion.42), channel_id=13, replica_groups=mesh['enc'=16,'dp'=2,'tensor'=4] {'enc'}, use_global_device_ids=true, to_apply=%region_35.39.clone | all-reduce | flops 49152 | bytes 294912
  411.9 0.6 gather_fusion.2
  412.7 0.7 gather_fusion.4
  413.5 0.2 broadcast_select_fusion
  413.6 0.4 slice_reduce_fusion.1
  414.7 15.1 %all-gather.9 = bf16[16,2,512]{2,1,0:T(2,128)(2,1)S(1)} all-gather(bf16[1,2,512]{2,1,0:T(2,128)(2,1)S(1)} %reshape.398), channel_id=1, replica_groups=mesh['enc'=16,'dp'=2,'tensor'=4] {'enc'}, dimensions={0}, use_global_device_ids=true | all-gather | bytes 34816 | tf_op jit(solution)/shard_map/all_gather | solution.py:131
  430.1 31.6 %all-gather.3 = f32[128,256]{1,0:T(8,128)S(1)} all-gather(f32[32,256]{1,0:T(8,128)S(1)} %fusion.116), channel_id=5, replica_groups=mesh['enc'=16,'dp'=2,'tensor'=4] {'tensor'}, dimensions={0}, use_global_device_ids=true | all-gather | bytes 163840 | tf_op jit(solution)/shard_map/all_gather | solution.py:40
  461.9 18.0 %all-gather.11 = bf16[16,2,512]{2,1,0:T(2,128)(2,1)S(1)} all-gather(bf16[1,2,512]{2,1,0:T(2,128)(2,1)S(1)} %reshape.402), channel_id=1, replica_groups=mesh['enc'=16,'dp'=2,'tensor'=4] {'enc'}, dimensions={0}, use_global_device_ids=true | all-gather | bytes 34816 | tf_op jit(solution)/shard_map/all_gather | solution.py:131
  480.0 0.1 fusion.119
  480.1 10.9 %all-gather.5 = f32[128,256]{1,0:T(8,128)S(1)} all-gather(f32[32,256]{1,0:T(8,128)S(1)} %fusion.119), channel_id=7, replica_groups=mesh['enc'=16,'dp'=2,'tensor'=4] {'tensor'}, dimensions={0}, use_global_device_ids=true | all-gather | bytes 163840 | tf_op jit(solution)/shard_map/all_gather | solution.py:40
  491.3 15.1 %all-gather.7 = bf16[16,2,512]{2,1,0:T(2,128)(2,1)S(1)} all-gather(bf16[1,2,512]{2,1,0:T(2,128)(2,1)S(1)} %reshape.394), channel_id=1, replica_groups=mesh['enc'=16,'dp'=2,'tensor'=4] {'enc'}, dimensions={0}, use_global_device_ids=true | all-gather | bytes 34816 | tf_op jit(solution)/shard_map/all_gather | solution.py:131
  506.4 0.1 fusion.113
  506.6 10.6 %all-gather.1 = f32[128,256]{1,0:T(8,128)S(1)} all-gather(f32[32,256]{1,0:T(8,128)S(1)} %fusion.113), channel_id=3, replica_groups=mesh['enc'=16,'dp'=2,'tensor'=4] {'tensor'}, dimensions={0}, use_global_device_ids=true | all-gather | bytes 163840 | tf_op jit(solution)/shard_map/all_gather | solution.py:40
  517.2 0.6 pad_maximum_fusion
  (115 shorter events, 4.0 us)
Async XLA Ops:
  0.0 43.5 %copy-start = (bf16[256,3,512]{2,0,1:T(8,128)(2,1)S(1)}, bf16[256,3,512]{2,0,1:T(8,128)(2,1)}, u32[]{:S(2)}) copy-start(bf16[256,3,512]{2,0,1:T(8,128)(2,1)} %param.25) | copy-start | bytes 2359300
  0.1 0.7 copy-start.1
  1.3 0.9 copy-start.9
  3.7 5.0 copy-start.7
  3.7 409.0 %all-to-all-start = ((bf16[2,24,2,512]{3,2,1,0:T(2,128)(2,1)}), bf16[2,24,2,512]{3,2,1,0:T(2,128)(2,1)S(1)}, u32[]{:S(2)}, u32[]{:S(2)}) async-start(bf16[2,24,2,512]{3,2,1,0:T(2,128)(2,1)} %broadcast_select_fusion.1), calls=%async_computation | async-start | bytes 196608 | tf_op jit(solution)/shard_map/all_to_all | solution.py:87
  43.5 0.7 copy-start.11
  101.6 0.7 copy-start.12
  103.5 0.7 copy-start.2
  104.1 0.8 copy-start.8
  104.8 16.3 %copy-start.4 = (bf16[512,256]{1,0:T(8,128)(2,1)S(1)}, bf16[512,256]{1,0:T(8,128)(2,1)}, u32[]{:S(2)}) copy-start(bf16[512,256]{1,0:T(8,128)(2,1)} %param.26) | copy-start | bytes 786436
  310.9 42.2 %copy-start.6 = (bf16[256,512]{1,0:T(8,128)(2,1)S(1)}, bf16[256,512]{1,0:T(8,128)(2,1)}, u32[]{:S(2)}) copy-start(bf16[256,512]{1,0:T(8,128)(2,1)} %param.28) | copy-start | bytes 786436
  353.1 0.7 copy-start.10
  354.4 57.5 %copy-start.3 = (s32[64]{0:T(128)S(1)}, s32[64]{0:T(128)}, u32[]{:S(2)}) copy-start(s32[64]{0:T(128)} %param.22) | copy-start | bytes 772
  414.0 15.9 %copy-start.5 = (bf16[512,256]{1,0:T(8,128)(2,1)S(1)}, bf16[512,256]{1,0:T(8,128)(2,1)}, u32[]{:S(2)}) copy-start(bf16[512,256]{1,0:T(8,128)(2,1)} %param.29) | copy-start | bytes 786436
